TPU v7x, 32 devices: a whole 2x2x4 slice. The times are simulated.
32 devices in a mesh: row: 4 (over x, core), col: 8 (over z, y).
Axes of the slice: x: 2, y: 2, z: 4, core: 2. Of those that a mesh axis runs over, the one named last changes fastest.
Arguments:
- amplitudes: float32 [8, 64, 512, 512], P(None, None, None, ('row', 'col')), may hold values from -6 to 6
- cycle_integrals: float32 [64, 512, 4, 512], P('col'), may hold values from -0.125 to 0.125
- occ_irrep: int32 [64], replicated, may hold values from 0 to 7
- virt_irrep: int32 [512], replicated, may hold values from 0 to 7
Outputs:
- cycle: float32 [8, 512, 2048], P(None, 'row', 'col')
All inputs are finite; a program needn't handle non-finite values.
Results may differ from a plain program's by a relative error of at most 0.0003.
Values sent between devices are 32-bit elements; how exact they have to be, the bound alone decides.
No kernel may reach another device: no remote copies, remote signals or barrier semaphores. Data moves between devices by JAX's collectives and lax.ppermute only.
A program may use at most 256 MiB of HBM per device.

v0:
```python
import jax
import jax.numpy as jnp
from jax import lax
from jax.sharding import PartitionSpec as P


def scatter_sum(flat, col_count, col_place):
    rows, a_local, width = flat.shape
    shard = width // col_count
    pairs_n = col_count // 2
    side = col_place % 2
    line = col_place // 2
    parts = flat.reshape(rows, a_local, pairs_n, 2, shard)
    keep = jnp.where(side == 0, parts[:, :, :, 0], parts[:, :, :, 1])
    give = jnp.where(side == 0, parts[:, :, :, 1], parts[:, :, :, 0])
    swap = [(q, q ^ 1) for q in range(col_count)]
    line_sum = keep + lax.ppermute(give, "col", swap)
    total = lax.dynamic_index_in_dim(line_sum, line, axis=2, keepdims=False)
    up_prev = None
    down_prev = None
    for t in range(pairs_n - 1):
        up_send = line_sum[:, :, t + 1 :]
        down_send = line_sum[:, :, : pairs_n - 1 - t]
        if up_prev is not None:
            up_send = up_send + up_prev[:, :, 1:]
            down_send = down_send + down_prev[:, :, :-1]
        payload = jnp.where(line == t, up_send, down_send)
        links = []
        for v in range(2):
            links.append((2 * t + v, 2 * (t + 1) + v))
            links.append((2 * (pairs_n - 1 - t) + v, 2 * (pairs_n - 2 - t) + v))
        got = lax.ppermute(payload, "col", links)
        up_prev = jnp.where(line == t + 1, got, 0.0)
        down_prev = jnp.where(line == pairs_n - 2 - t, got, 0.0)
        total = total + up_prev[:, :, 0] + down_prev[:, :, -1]
    return total


def per_device(amplitudes, cycle_integrals, occ_irrep, virt_irrep):
    slab_rows, occ_count, virt_count, c_local = amplitudes.shape
    col_count = lax.axis_size("col")
    row_count = lax.axis_size("row")
    k_local = occ_count // col_count
    a_local = virt_count // row_count
    column_slab = cycle_integrals.shape[2]
    col_place = lax.axis_index("col")
    row_place = lax.axis_index("row")
    k_irrep = lax.dynamic_slice_in_dim(occ_irrep, col_place * k_local, k_local)
    c_irrep = lax.dynamic_slice_in_dim(
        virt_irrep, (row_place * col_count + col_place) * c_local, c_local
    )
    slab_irrep = occ_irrep[:slab_rows]
    column_irrep = occ_irrep[:column_slab]
    int_sym = (
        k_irrep[:, None, None, None]
        ^ virt_irrep[None, :, None, None]
        ^ (column_irrep[None, None, :, None] ^ virt_irrep[None, None, None, :])
    )
    masked_ints = jnp.where(int_sym == 0, cycle_integrals, 0.0).reshape(
        k_local * virt_count, column_slab * virt_count
    )
    chunks = 2 if slab_rows % 2 == 0 else 1
    rows = slab_rows // chunks
    results = []
    for step in range(chunks):
        amps = amplitudes[step * rows : (step + 1) * rows]
        amp_sym = (
            slab_irrep[step * rows : (step + 1) * rows, None, None, None]
            ^ occ_irrep[None, :, None, None]
            ^ (virt_irrep[None, None, :, None] ^ c_irrep[None, None, None, :])
        )
        masked_amps = jnp.where(amp_sym == 0, amps, 0.0)
        grouped = masked_amps.reshape(rows, col_count, k_local, row_count, a_local, c_local)
        grouped = jnp.transpose(grouped, (0, 3, 1, 2, 4, 5)).reshape(
            rows, row_count * col_count, k_local, a_local, c_local
        )
        if step == 1 and chunks > 2:
            grouped, masked_ints = lax.optimization_barrier((grouped, masked_ints))
        if step >= 2:
            grouped, results[step - 2] = lax.optimization_barrier((grouped, results[step - 2]))
        items = lax.all_to_all(grouped, ("row", "col"), split_axis=1, concat_axis=4, tiled=True)
        blocks = jnp.transpose(items.reshape(rows, k_local, a_local, virt_count), (0, 2, 1, 3))
        blocks = blocks.reshape(rows, a_local, k_local * virt_count)
        partial_value = jnp.einsum(
            "iap,pq->iaq",
            blocks,
            masked_ints,
            precision=lax.Precision.HIGH,
            preferred_element_type=jnp.float32,
        )
        flat = partial_value.reshape(rows, a_local, column_slab * virt_count)
        results.append(lax.psum_scatter(flat, "col", scatter_dimension=2, tiled=True))
    return jnp.concatenate(results, axis=0)


def solution(mesh):
    placed = (P(None, None, None, ("row", "col")), P("col", None, None, None), P(), P())
    return jax.shard_map(
        per_device, mesh=mesh, in_specs=placed, out_specs=P(None, "row", "col"), check_vma=False
    )
```

profile of v0, /device:TPU:0, one launch (start us, length us, event | category | flops | bytes accessed | tf_op | source)
XLA Modules:
  0.0 593.7 jit_solution(1753503171140539836)
XLA Ops:
  6.5 0.8 fusion.1
  7.3 0.8 dynamic_slice.6
  8.1 0.8 broadcast_xor_fusion
  8.8 0.7 broadcast_xor_fusion.4
  9.6 11.0 %slice_select_fusion.1 = (f32[4,64,512,16]{2,3,1,0:T(8,128)}, f32[4,64,512,16]{2,3,1,0:T(8,128)}) fusion(f32[8,64,512,16]{2,3,1,0:T(8,128)} %param.4, s32[512,16]{0,1:T(8,128)S(1)} %broadcast_xor_fusion, s32[4,64]{1,0:T(4,128)S(1)} %get-tuple-element.7, s32[4,64]{1,0:T(4,128)S(1)} %get-tuple-element.8), kind=kLoop, calls=%fused_computation.4 | loop fusion | flops 12582912 | bytes 33589248 | tf_op jit(solution)/shard_map/jit(_where)/select_n | solution.py:72
  20.6 9.9 %reshape.185 = f32[4,8,8,4,128,16]{4,3,5,2,1,0:T(4,128)} reshape(f32[4,64,512,16]{2,3,1,0:T(8,128)} %get-tuple-element.5) | data formatting | bytes 16777216 | tf_op jit(solution)/shard_map/reshape | solution.py:73
  30.5 7.8 %copy.23 = f32[4,4,8,8,128,16]{4,5,3,0,2,1:T(8,128)} copy(f32[4,4,8,8,128,16]{4,1,5,3,2,0:T(4,128)} %bitcast.38) | data formatting | bytes 16777216 | tf_op jit(solution)/shard_map/reshape | solution.py:74
  38.3 7.4 %all-to-all-start = ((f32[4,32,8,128,16]{3,4,2,0,1:T(8,128)}), f32[4,32,8,128,16]{3,4,2,0,1:T(8,128)}, u32[]{:S(2)}, u32[]{:S(2)}) async-start(f32[4,32,8,128,16]{3,4,2,0,1:T(8,128)} %bitcast.37), calls=%async_computation | async-start | bytes 16777216 | tf_op jit(solution)/shard_map/all_to_all | solution.py:81
  45.7 9.9 %reshape.190 = f32[4,8,8,4,128,16]{4,3,5,2,1,0:T(4,128)} reshape(f32[4,64,512,16]{2,3,1,0:T(8,128)} %get-tuple-element.6) | data formatting | bytes 16777216 | tf_op jit(solution)/shard_map/reshape | solution.py:73
  55.7 7.9 %copy.25 = f32[4,4,8,8,128,16]{4,5,3,0,2,1:T(8,128)} copy(f32[4,4,8,8,128,16]{4,1,5,3,2,0:T(4,128)} %bitcast.39) | data formatting | bytes 16777216 | tf_op jit(solution)/shard_map/reshape | solution.py:74
  63.5 171.8 %all-to-all-done = f32[4,32,8,128,16]{3,4,2,0,1:T(8,128)} async-done(((f32[4,32,8,128,16]{3,4,2,0,1:T(8,128)}), f32[4,32,8,128,16]{3,4,2,0,1:T(8,128)}, u32[]{:S(2)}, u32[]{:S(2)}) %all-to-all-start) | async-done | bytes 8388640 | tf_op jit(solution)/shard_map/all_to_all | solution.py:81
  235.3 3.8 all-to-all-start.1
  239.1 0.2 reduce-scatter.3.cloned.1.call-start
  239.3 0.1 dynamic_slice.7
  239.6 23.1 %fusion = f32[8,512,4,512]{3,2,1,0:T(4,128)} fusion(f32[8,512,4,512]{3,2,1,0:T(4,128)} %param.5, s32[4,512]{1,0:T(4,128)S(1)} %broadcast_xor_fusion.2, s32[8,512]{1,0:T(8,128)S(1)} %broadcast_xor_fusion.1), kind=kLoop, calls=%fused_computation.1 | loop fusion | flops 25165824 | bytes 67133440 | tf_op jit(solution)/shard_map/jit(_where)/select_n | solution.py:59
  262.7 39.8 %reshape.194 = f32[4096,2048,1]{1,0,2:T(8,128)} reshape(f32[8,512,4,512]{3,2,1,0:T(4,128)} %fusion) | data formatting | bytes 67108864 | tf_op jit(solution)/shard_map/reshape | solution.py:59
  302.4 4.5 copy.17
  307.0 32.7 %fusion.2 = f32[4,128,2048]{2,1,0:T(8,128)} fusion(f32[4,128,4096]{1,2,0:T(8,128)S(1)} %bitcast.41, f32[4096,2048,1]{1,0,2:T(8,128)} %reshape.194), kind=kOutput, calls=%fused_computation.13 | convolution fusion | flops 25769803776 | bytes 46137344 | tf_op jit(solution)/shard_map/iap,pq->iaq/dot_general | solution.py:84
  339.8 0.3 reduce-scatter.5.cloned.1.call-start
  340.0 122.3 %all-to-all-done.1 = f32[4,32,8,128,16]{3,4,2,0,1:T(8,128)} async-done(((f32[4,32,8,128,16]{3,4,2,0,1:T(8,128)}), f32[4,32,8,128,16]{3,4,2,0,1:T(8,128)}, u32[]{:S(2)}, u32[]{:S(2)}) %all-to-all-start.1) | async-done | bytes 8388640 | tf_op jit(solution)/shard_map/all_to_all | solution.py:81
  462.3 4.5 copy.21
  466.9 33.0 %fusion.3 = f32[4,128,2048]{2,1,0:T(8,128)} fusion(f32[4,128,4096]{1,2,0:T(8,128)S(1)} %bitcast.40, f32[4096,2048,1]{1,0,2:T(8,128)} %reshape.194), kind=kOutput, calls=%fused_computation.14 | convolution fusion | flops 25769803776 | bytes 46137344 | tf_op jit(solution)/shard_map/iap,pq->iaq/dot_general | solution.py:84
  499.9 84.6 %reduce-scatter.5.cloned.1.call-done = f32[4,128,256]{2,1,0:T(8,128)} async-done(((f32[4,128,2048]{2,1,0:T(8,128)}), f32[4,128,256]{2,1,0:T(8,128)}) %reduce-scatter.5.cloned.1.call-update) | async-done | bytes 524304 | tf_op jit(solution)/shard_map/reduce_scatter | solution.py:92
  584.6 2.2 pad_maximum_fusion
  (9 shorter events, 0.2 us)
Async XLA Ops:
  38.3 197.0 %all-to-all-start = ((f32[4,32,8,128,16]{3,4,2,0,1:T(8,128)}), f32[4,32,8,128,16]{3,4,2,0,1:T(8,128)}, u32[]{:S(2)}, u32[]{:S(2)}) async-start(f32[4,32,8,128,16]{3,4,2,0,1:T(8,128)} %bitcast.37), calls=%async_computation | async-start | bytes 16777216 | tf_op jit(solution)/shard_map/all_to_all | solution.py:81
  235.3 4.1 copy-start.1
  235.3 4.1 copy-start
  235.3 227.0 %all-to-all-start.1 = ((f32[4,32,8,128,16]{3,4,2,0,1:T(8,128)}), f32[4,32,8,128,16]{3,4,2,0,1:T(8,128)}, u32[]{:S(2)}, u32[]{:S(2)}) async-start(f32[4,32,8,128,16]{3,4,2,0,1:T(8,128)} %bitcast.36), calls=%async_computation.2 | async-start | bytes 16777216 | tf_op jit(solution)/shard_map/all_to_all | solution.py:81
  239.1 260.8 %reduce-scatter.3.cloned.1.call-start = ((), (), s32[]{:S(2)}) async-start(), calls=%async_computation.4 | async-start | bytes 4718592 | tf_op jit(solution)/shard_map/reduce_scatter | solution.py:92
  339.8 244.8 %reduce-scatter.5.cloned.1.call-start = ((), (), s32[]{:S(2)}) async-start(), calls=%async_computation.5 | async-start | bytes 4718592 | tf_op jit(solution)/shard_map/reduce_scatter | solution.py:92
Sparse Core Ops, SparseCore 0:
  339.9 149.7 reduce-scatter.2
  500.0 84.4 reduce-scatter.4
where the time goes:
time: 596 us; the launch traced here: 594 us
  waiting for transfers between devices  379 us (64%)
  local copies, waits for them, and re-layouts  86 us (14%)
  matrix products  65.8 us (11%)
  other arithmetic  38 us (6%)
  between operations  13.5 us (2%)
  starting transfers between devices  11.7 us (2%)
    all_to_all x2, waiting for transfers between devices, per_device(): lax.all_to_all(grouped, ('row', 'col'), split_axis=1, concat_axis=4, tile...  294 us
    reduce_scatter x2, waiting for transfers between devices, per_device(): lax.psum_scatter(flat, 'col', scatter_dimension=2, tiled=True)  84.6 us
    dot_general x2, matrix products, per_device(): jnp.einsum('iap,pq->iaq', blocks, masked_ints, precision=lax.Precision.HI...  65.8 us
    reshape x1, local copies, waits for them, and re-layouts, per_device(): jnp.where(int_sym == 0, cycle_integrals, 0.0)  39.8 us
    select_n x1, other arithmetic, per_device(): jnp.where(int_sym == 0, cycle_integrals, 0.0)  23.1 us
    reshape x2, local copies, waits for them, and re-layouts, per_device(): masked_amps.reshape(rows, col_count, k_local, row_count, a_local, c_local)  19.8 us
    reshape x2, local copies, waits for them, and re-layouts, per_device(): jnp.transpose(grouped, (0, 3, 1, 2, 4, 5))  15.6 us
  transfers between devices with their start and end apart: 4, of which 3 were waited for; matrix products, arithmetic and copies ran while one was open for 26% of the time, Pallas kernels for 0%

commit v1 on v0

--- a/solution.py
+++ b/solution.py
@@ -78,7 +78,15 @@
             grouped, masked_ints = lax.optimization_barrier((grouped, masked_ints))
         if step >= 2:
             grouped, results[step - 2] = lax.optimization_barrier((grouped, results[step - 2]))
-        items = lax.all_to_all(grouped, ("row", "col"), split_axis=1, concat_axis=4, tiled=True)
+        items = jnp.concatenate(
+            lax.all_to_all(
+                jnp.stack(jnp.split(grouped, lax.axis_size(("row", "col")), axis=1)),
+                ("row", "col"),
+                0,
+                0,
+            ),
+            axis=4,
+        )
         blocks = jnp.transpose(items.reshape(rows, k_local, a_local, virt_count), (0, 2, 1, 3))
         blocks = blocks.reshape(rows, a_local, k_local * virt_count)
         partial_value = jnp.einsum(

time: 596 us -> 622 us (1.044)
  local copies, waits for them, and re-layouts: 86 us -> 139 us
  waiting for transfers between devices: 379 us -> 353 us
    unnamed x4 -> x70, local copies, waits for them, and re-layouts: 0.01 us -> 47 us
    all_to_all x2, waiting for transfers between devices: 294 us -> 268 us  [per_device(): lax.all_to_all(jnp.stack(jnp.split(grouped, lax.axis_size(('row', 'col'))...]
    reshape x0 -> x2, local copies, waits for them, and re-layouts: none -> 9.07 us  [per_device(): jnp.concatenate(lax.all_to_all(jnp.stack(jnp.split(grouped, lax.axis_size...]
    all_to_all x2 -> x0, local copies, waits for them, and re-layouts: 9.07 us -> none  [per_device(): lax.all_to_all(grouped, ('row', 'col'), split_axis=1, concat_axis=4, tile...]
    transpose x0 -> x2, local copies, waits for them, and re-layouts: none -> 8.81 us  [per_device(): jnp.transpose(grouped, (0, 3, 1, 2, 4, 5))]
    reshape x2, local copies, waits for them, and re-layouts: 15.6 us -> 9.38 us  [per_device(): jnp.transpose(grouped, (0, 3, 1, 2, 4, 5))]
  transfers between devices with their start and end apart: 4 -> 4, of which waited for: 3 -> 3; matrix products, arithmetic and copies ran while one was open for 26% -> 29% of each run, Pallas kernels for 0% -> 0%
where the time goes in v1:
time: 622 us; the launch traced here: 620 us
  waiting for transfers between devices  353 us (57%)
  local copies, waits for them, and re-layouts  139 us (22%)
  matrix products  65.7 us (11%)
  other arithmetic  38 us (6%)
  between operations  13.5 us (2%)
  starting transfers between devices  11.6 us (2%)
    all_to_all x2, waiting for transfers between devices, per_device(): lax.all_to_all(jnp.stack(jnp.split(grouped, lax.axis_size(('row', 'col'))...  268 us
    reduce_scatter x2, waiting for transfers between devices, per_device(): lax.psum_scatter(flat, 'col', scatter_dimension=2, tiled=True)  84.8 us
    dot_general x2, matrix products, per_device(): jnp.einsum('iap,pq->iaq', blocks, masked_ints, precision=lax.Precision.HI...  65.7 us
    unnamed x70, local copies, waits for them, and re-layouts  47 us
    reshape x1, local copies, waits for them, and re-layouts, per_device(): jnp.where(int_sym == 0, cycle_integrals, 0.0)  39.8 us
    select_n x1, other arithmetic, per_device(): jnp.where(int_sym == 0, cycle_integrals, 0.0)  23.1 us
    reshape x2, local copies, waits for them, and re-layouts, per_device(): masked_amps.reshape(rows, col_count, k_local, row_count, a_local, c_local)  19.8 us
  transfers between devices with their start and end apart: 4, of which 3 were waited for; matrix products, arithmetic and copies ran while one was open for 29% of the time, Pallas kernels for 0%

profile of v1, /device:TPU:0, one launch (start us, length us, event | category | flops | bytes accessed | tf_op | source)
XLA Modules:
  0.0 620.3 jit_solution(3226192076454397473)
XLA Ops:
  6.5 0.8 fusion.65
  9.6 11.0 %slice_select_fusion.1 = (f32[4,64,512,16]{2,3,1,0:T(8,128)}, f32[4,64,512,16]{2,3,1,0:T(8,128)}) fusion(f32[8,64,512,16]{2,3,1,0:T(8,128)} %param.4, s32[512,16]{0,1:T(8,128)S(1)} %broadcast_xor_fusion, s32[4,64]{1,0:T(4,128)S(1)} %get-tuple-element.7, s32[4,64]{1,0:T(4,128)S(1)} %get-tuple-element.8), kind=kLoop, calls=%fused_computation.4 | loop fusion | flops 12582912 | bytes 33589248 | tf_op jit(solution)/shard_map/jit(_where)/select_n | solution.py:72
  20.6 9.9 %reshape.183 = f32[4,8,8,4,128,16]{4,3,5,2,1,0:T(4,128)} reshape(f32[4,64,512,16]{2,3,1,0:T(8,128)} %get-tuple-element.5) | data formatting | bytes 16777216 | tf_op jit(solution)/shard_map/reshape | solution.py:73
  30.5 4.7 copy.201
  35.2 1.1 copy-done
  36.3 4.4 copy.133
  63.2 1.7 fusion.33
  64.9 7.4 %all-to-all-start = ((f32[32,4,1,8,128,16]{4,5,3,1,2,0:T(8,128)}), f32[32,4,1,8,128,16]{4,5,3,1,2,0:T(8,128)}, u32[]{:S(2)}, u32[]{:S(2)}) async-start(f32[32,4,1,8,128,16]{4,5,3,1,2,0:T(8,128)} %fusion.33), calls=%async_computation | async-start | bytes 16777216 | tf_op jit(solution)/shard_map/all_to_all | solution.py:82
  72.3 9.9 %reshape.188 = f32[4,8,8,4,128,16]{4,3,5,2,1,0:T(4,128)} reshape(f32[4,64,512,16]{2,3,1,0:T(8,128)} %get-tuple-element.6) | data formatting | bytes 16777216 | tf_op jit(solution)/shard_map/reshape | solution.py:73
  82.2 4.7 copy.233
  86.9 1.1 copy-done.1
  88.0 4.4 copy.167
  114.8 1.7 fusion.1
  116.4 145.4 %all-to-all-done = f32[32,4,1,8,128,16]{4,5,3,1,2,0:T(8,128)} async-done(((f32[32,4,1,8,128,16]{4,5,3,1,2,0:T(8,128)}), f32[32,4,1,8,128,16]{4,5,3,1,2,0:T(8,128)}, u32[]{:S(2)}, u32[]{:S(2)}) %all-to-all-start) | async-done | bytes 8388640 | tf_op jit(solution)/shard_map/all_to_all | solution.py:82
  261.9 3.7 all-to-all-start.1
  266.0 23.1 %fusion = f32[8,512,4,512]{3,2,1,0:T(4,128)} fusion(f32[8,512,4,512]{3,2,1,0:T(4,128)} %param.5, s32[4,512]{1,0:T(4,128)S(1)} %broadcast_xor_fusion.2, s32[8,512]{1,0:T(8,128)S(1)} %broadcast_xor_fusion.1), kind=kLoop, calls=%fused_computation.1 | loop fusion | flops 25165824 | bytes 67133440 | tf_op jit(solution)/shard_map/jit(_where)/select_n | solution.py:59
  289.1 39.8 %reshape.192 = f32[4096,2048,1]{1,0,2:T(8,128)} reshape(f32[8,512,4,512]{3,2,1,0:T(4,128)} %fusion) | data formatting | bytes 67108864 | tf_op jit(solution)/shard_map/reshape | solution.py:59
  328.9 4.5 copy.165
  333.5 32.6 %fusion.66 = f32[4,128,2048]{2,1,0:T(8,128)} fusion(f32[4,128,4096]{1,2,0:T(8,128)S(1)} %bitcast.415, f32[4096,2048,1]{1,0,2:T(8,128)} %reshape.192), kind=kOutput, calls=%fused_computation.141 | convolution fusion | flops 25769803776 | bytes 46137344 | tf_op jit(solution)/shard_map/iap,pq->iaq/dot_general | solution.py:92
  366.4 122.4 %all-to-all-done.1 = f32[32,4,1,8,128,16]{4,5,3,1,2,0:T(8,128)} async-done(((f32[32,4,1,8,128,16]{4,5,3,1,2,0:T(8,128)}), f32[32,4,1,8,128,16]{4,5,3,1,2,0:T(8,128)}, u32[]{:S(2)}, u32[]{:S(2)}) %all-to-all-start.1) | async-done | bytes 8388640 | tf_op jit(solution)/shard_map/all_to_all | solution.py:82
  488.8 4.5 copy.199
  493.3 33.0 %fusion.67 = f32[4,128,2048]{2,1,0:T(8,128)} fusion(f32[4,128,4096]{1,2,0:T(8,128)S(1)} %bitcast.414, f32[4096,2048,1]{1,0,2:T(8,128)} %reshape.192), kind=kOutput, calls=%fused_computation.142 | convolution fusion | flops 25769803776 | bytes 46137344 | tf_op jit(solution)/shard_map/iap,pq->iaq/dot_general | solution.py:92
  526.4 84.8 %reduce-scatter.5.cloned.1.call-done = f32[4,128,256]{2,1,0:T(8,128)} async-done(((f32[4,128,2048]{2,1,0:T(8,128)}), f32[4,128,256]{2,1,0:T(8,128)}) %reduce-scatter.5.cloned.1.call-update) | async-done | bytes 524304 | tf_op jit(solution)/shard_map/reduce_scatter | solution.py:100
  611.2 2.2 pad_maximum_fusion
  (79 shorter events, 47.8 us)
Async XLA Ops:
  30.5 5.8 copy-start
  64.9 197.0 %all-to-all-start = ((f32[32,4,1,8,128,16]{4,5,3,1,2,0:T(8,128)}), f32[32,4,1,8,128,16]{4,5,3,1,2,0:T(8,128)}, u32[]{:S(2)}, u32[]{:S(2)}) async-start(f32[32,4,1,8,128,16]{4,5,3,1,2,0:T(8,128)} %fusion.33), calls=%async_computation | async-start | bytes 16777216 | tf_op jit(solution)/shard_map/all_to_all | solution.py:82
  82.2 5.8 copy-start.1
  116.4 149.4 %copy-start.3 = (s32[64]{0:T(128)S(1)}, s32[64]{0:T(128)}, u32[]{:S(2)}) copy-start(s32[64]{0:T(128)} %param.6) | copy-start | bytes 772
  116.4 149.4 %copy-start.2 = (s32[512]{0:T(512)S(1)}, s32[512]{0:T(512)}, u32[]{:S(2)}) copy-start(s32[512]{0:T(512)} %param.7) | copy-start | bytes 6148
  261.9 226.9 %all-to-all-start.1 = ((f32[32,4,1,8,128,16]{4,5,3,1,2,0:T(8,128)}), f32[32,4,1,8,128,16]{4,5,3,1,2,0:T(8,128)}, u32[]{:S(2)}, u32[]{:S(2)}) async-start(f32[32,4,1,8,128,16]{4,5,3,1,2,0:T(8,128)} %fusion.1), calls=%async_computation.2 | async-start | bytes 16777216 | tf_op jit(solution)/shard_map/all_to_all | solution.py:82
  265.6 260.8 %reduce-scatter.3.cloned.1.call-start = ((), (), s32[]{:S(2)}) async-start(), calls=%async_computation.4 | async-start | bytes 4718592 | tf_op jit(solution)/shard_map/reduce_scatter | solution.py:100
  366.1 245.1 %reduce-scatter.5.cloned.1.call-start = ((), (), s32[]{:S(2)}) async-start(), calls=%async_computation.5 | async-start | bytes 4718592 | tf_op jit(solution)/shard_map/reduce_scatter | solution.py:100
Sparse Core Ops, SparseCore 0:
  366.2 149.8 reduce-scatter.2
  526.5 84.6 reduce-scatter.4
